TPU v7x, 32 devices: a whole 2x2x4 slice. The times are simulated.
32 devices in a mesh: sec: 4 (over y, x), dev: 8 (over z, core).
Axes of the slice: x: 2, y: 2, z: 4, core: 2. Of those that a mesh axis runs over, the one named last changes fastest.
Arguments:
- strain_rows: bfloat16 [65536, 128], P(('sec', 'dev')), may hold values from -6 to 6
- bands: int32 [65536], P(('sec', 'dev')), may hold values from 0 to 15
- damaged: int32 [4096], P(('sec', 'dev')), may hold values from 0 to 2047
- owner: int32 [4096, 1], P(('sec', 'dev')), may hold values from 0 to 31; in each aligned block of 128 rows (0 to 127, 128 to 255, ...) at most 8 rows name the same one
- first_layers: bfloat16 [4096, 4096], P(('sec', 'dev')), may hold values from -0.5 to 0.5
- middle_weight: bfloat16 [4096, 4096], P(None, 'sec'), may hold values from -0.09375 to 0.09375
- out_weight: bfloat16 [4096, 128], P('sec'), may hold values from -0.09375 to 0.09375
- band_scale: float32 [16, 4096], replicated, may hold values from 0.5 to 2
- back_weight: bfloat16 [128, 128], replicated, may hold values from -0.5 to 0.5
Outputs:
- response: bfloat16 [4096, 128], P(('sec', 'dev'))
Inputs may be any that keep to these rules, and one draw needn't show every extreme that they name: Among the 128 rows of one macro device no owner is named more than 8 times, a bound that some block reaches. `damaged`: indices into the listing device's own 2048 points.
All inputs are finite; a program needn't handle non-finite values.
Results may differ from a plain program's by a relative error of at most 0.014.
Values may be sent and summed in bfloat16 or wider, within the bound.
No kernel may reach another device: no remote copies, remote signals or barrier semaphores. Data moves between devices by JAX's collectives and lax.ppermute only.
A program may use at most 128 MiB of HBM per device.

v0:
```python
import jax
import jax.numpy as jnp
from jax import lax
from jax.sharding import PartitionSpec as P

PASSES = 2


def scale_parts(band_scale):
    hi = band_scale.astype(jnp.bfloat16)
    rest = band_scale - hi.astype(jnp.float32)
    mid = rest.astype(jnp.bfloat16)
    lo = (rest - mid.astype(jnp.float32)).astype(jnp.bfloat16)
    return jnp.concatenate([hi, mid, lo], axis=0)


def band_rows(band_values, parts):
    levels = parts.shape[0] // 3
    level_ids = jnp.arange(3 * levels, dtype=jnp.int32) % levels
    picks = (band_values[:, None] == level_ids[None, :]).astype(jnp.bfloat16)
    return jnp.dot(picks, parts, preferred_element_type=jnp.float32)


def first_hidden(rows, weights, band_values, parts):
    mixed = jnp.einsum("srf,sfh->srh", rows, weights, preferred_element_type=jnp.float32)
    mixed = mixed.reshape(-1, weights.shape[2]) * band_rows(band_values, parts)
    return jax.nn.silu(mixed).astype(jnp.bfloat16)


def surrogate_tail(hidden_block, middle_weight, out_weight):
    middle = jax.nn.silu(
        jnp.dot(hidden_block, middle_weight, preferred_element_type=jnp.float32)
    ).astype(jnp.bfloat16)
    return jnp.dot(middle, out_weight, preferred_element_type=jnp.float32)


def per_device(
    strain_rows,
    bands,
    damaged,
    owner,
    first_layers,
    middle_weight,
    out_weight,
    band_scale,
    back_weight,
):
    n_sec = lax.axis_size("sec")
    n_dev = lax.axis_size("dev")
    count_all = n_sec * n_dev
    list_rows = damaged.shape[0]
    slot_count = max(2, 2 * list_rows // count_all)
    group_slots = n_sec * slot_count
    feat_width = strain_rows.shape[1]
    hid = first_layers.shape[1]
    every_first = lax.all_gather(first_layers, "sec", axis=0, tiled=True).reshape(
        n_sec, feat_width, hid
    )
    parts = scale_parts(band_scale)
    features = jnp.take(strain_rows, damaged, axis=0)
    band_local = jnp.take(bands, damaged)
    target_owner = owner[:, 0]
    matches = (target_owner[:, None] == jnp.arange(count_all, dtype=jnp.int32)[None, :]).astype(
        jnp.int32
    )
    slot_rank = jnp.sum((jnp.cumsum(matches, axis=0) - 1) * matches, axis=1)
    owner_sec = target_owner // n_dev
    owner_dev = target_owner % n_dev
    target = owner_dev * group_slots + owner_sec * slot_count + slot_rank
    dispatch = (
        jnp.arange(n_dev * group_slots, dtype=jnp.int32)[:, None] == target[None, :]
    ).astype(jnp.bfloat16)
    packed = jnp.concatenate([features, band_local.astype(jnp.bfloat16)[:, None]], axis=1)
    send = jnp.dot(dispatch, packed, preferred_element_type=jnp.float32).astype(jnp.bfloat16)
    send = send.reshape(1, n_dev, group_slots, feat_width + 1)
    send = jnp.broadcast_to(send, (n_sec, n_dev, group_slots, feat_width + 1)).reshape(
        count_all, group_slots, feat_width + 1
    )
    got = lax.all_to_all(send, ("sec", "dev"), split_axis=0, concat_axis=0, tiled=True)
    got = got.reshape(count_all, n_sec, slot_count, feat_width + 1).transpose(1, 0, 2, 3)
    got = got.reshape(n_sec, count_all * slot_count, feat_width + 1)
    rows = got[:, :, :feat_width]
    got_band = got[:, :, feat_width].astype(jnp.int32).reshape(-1)
    result = None
    for segment_index in range(PASSES):
        hidden = first_hidden(rows, every_first, got_band, parts)
        partial = surrogate_tail(hidden, middle_weight, out_weight)
        if segment_index + 1 < PASSES:
            values = lax.psum(partial, "sec").astype(jnp.bfloat16)
            rows = (
                rows.astype(jnp.float32)
                + jnp.dot(values, back_weight, preferred_element_type=jnp.float32).reshape(
                    rows.shape
                )
            ).astype(jnp.bfloat16)
        else:
            out_width = partial.shape[1]
            back = partial.reshape(n_sec, count_all, slot_count, out_width).transpose(1, 0, 2, 3)
            back = lax.all_to_all(back, ("sec", "dev"), split_axis=0, concat_axis=0, tiled=True)
            back = back.reshape(n_sec, n_dev * group_slots, out_width).sum(axis=0)
            result = jnp.take(back, target, axis=0).astype(jnp.bfloat16)
    return result


def solution(mesh):
    in_specs = (
        P(("sec", "dev"), None),
        P(("sec", "dev")),
        P(("sec", "dev")),
        P(("sec", "dev"), None),
        P(("sec", "dev"), None),
        P(None, "sec"),
        P("sec", None),
        P(),
        P(),
    )
    out_specs = P(("sec", "dev"), None)
    return jax.shard_map(
        per_device, mesh=mesh, in_specs=in_specs, out_specs=out_specs, check_vma=False
    )
```

profile of v0, /device:TPU:0, one launch (start us, length us, event | category | flops | bytes accessed | tf_op | source)
XLA Modules:
  0.0 186.2 jit_solution(1819267888237272443)
XLA Ops:
  6.5 0.7 all-gather.2.cloned.1.call-update
  7.9 1.6 gather_fusion.1
  9.6 0.7 gather_fusion
  10.3 0.7 convert_bitcast_fusion
  11.1 0.7 fusion.22
  12.0 0.8 select_reduce_fusion
  12.8 0.7 fusion.28
  13.9 0.8 broadcast_in_dim.47
  14.8 7.3 %all-to-all-start = ((bf16[32,32,129]{2,1,0:T(8,128)(2,1)}), bf16[32,32,129]{2,1,0:T(8,128)(2,1)S(1)}, u32[]{:S(2)}, u32[]{:S(2)}) async-start(bf16[32,32,129]{2,1,0:T(8,128)(2,1)} %bitcast.5), calls=%async_computation | async-start | bytes 1048576 | tf_op jit(solution)/shard_map/all_to_all | solution.py:79
  22.1 1.1 fusion.33
  23.2 15.2 %all-to-all-done = bf16[32,32,129]{2,1,0:T(8,128)(2,1)S(1)} async-done(((bf16[32,32,129]{2,1,0:T(8,128)(2,1)}), bf16[32,32,129]{2,1,0:T(8,128)(2,1)S(1)}, u32[]{:S(2)}, u32[]{:S(2)}) %all-to-all-start) | async-done | bytes 264224 | tf_op jit(solution)/shard_map/all_to_all | solution.py:79
  38.7 31.4 %all-gather.2.cloned.1.call-done = bf16[512,4096]{1,0:T(8,128)(2,1)} async-done(((bf16[128,4096]{1,0:T(8,128)(2,1)}), bf16[512,4096]{1,0:T(8,128)(2,1)}) %all-gather.2.cloned.1.call-update) | async-done | bytes 4194320 | tf_op jit(solution)/shard_map/all_gather | solution.py:56
  70.1 4.5 %fusion.14 = f32[4,256,4096]{2,1,0:T(8,128)S(1)} fusion(bf16[4,128,4096]{2,1,0:T(8,128)(2,1)} %bitcast.48, bf16[4,256,129]{2,1,0:T(8,128)(2,1)S(1)} %copy_bitcast_fusion.1), kind=kOutput, calls=%fused_computation.30 | convolution fusion | flops 1073741824 | bytes 21233664 | tf_op jit(solution)/shard_map/srf,sfh->srh/dot_general | solution.py:25
  74.7 10.1 %multiply_convert_fusion.1 = (bf16[1024,4096]{1,0:T(8,128)(2,1)}, f32[1024,4096]{1,0:T(8,128)}) fusion(f32[4,256,4096]{2,1,0:T(8,128)S(1)} %fusion.14, bf16[16,4096]{1,0:T(8,128)(2,1)S(1)} %get-tuple-element.10, bf16[16,4096]{1,0:T(8,128)(2,1)S(1)} %get-tuple-element.11, bf16[16,4096]{1,0:T(8,128)(2,1)S(1)} %get-tuple-element.9, s32[48]{0:T(128)S(1)} %and_select_fusion, ...), kind=kOutput, calls=%fused_computation.6 | convolution fusion | flops 429047808 | bytes 42340544 | tf_op jit(solution)/shard_map/dot_general | solution.py:21
  84.8 14.5 %fusion = f32[1024,128]{1,0:T(8,128)S(1)} fusion(bf16[1024,128]{1,0:T(8,128)(2,1)S(1)} %copy-done.4, bf16[1024,4096]{1,0:T(8,128)(2,1)} %get-tuple-element.12, bf16[4096,1024]{1,0:T(8,128)(2,1)} %param.14), kind=kOutput, calls=%fused_computation.9 | convolution fusion | flops 8863612928 | bytes 17563648 | tf_op jit(solution)/shard_map/dot_general | solution.py:34
  99.3 27.1 %all-reduce.1 = bf16[1024,128]{1,0:T(8,128)(2,1)S(1)} all-reduce(f32[1024,128]{1,0:T(8,128)S(1)} %fusion), channel_id=1, replica_groups=mesh['sec'=4,'dev'=8] {'sec'}, use_global_device_ids=true, to_apply=%region_2.3 | all-reduce | flops 131072 | bytes 786432 | tf_op jit(solution)/shard_map/psum | solution.py:89
  126.6 4.5 %fusion.9 = f32[4,256,4096]{2,1,0:T(8,128)S(1)} fusion(bf16[4,128,4096]{2,1,0:T(8,128)(2,1)} %bitcast.49, f32[4,256,128]{2,1,0:T(8,128)S(1)} %bitcast.50, bf16[4,256,129]{2,1,0:T(8,128)(2,1)S(1)} %copy_bitcast_fusion.1), kind=kOutput, calls=%fused_computation.23 | convolution fusion | flops 1074135040 | bytes 21757952 | tf_op jit(solution)/shard_map/srf,sfh->srh/dot_general | solution.py:25
  131.1 10.9 %multiply_convert_fusion = bf16[1024,4096]{1,0:T(8,128)(2,1)} fusion(f32[1024,4096]{1,0:T(8,128)} %get-tuple-element.13, f32[4,256,4096]{2,1,0:T(8,128)S(1)} %fusion.9), kind=kLoop, calls=%fused_computation.5 | loop fusion | flops 25165824 | bytes 41943040 | tf_op jit(solution)/shard_map/convert_element_type | solution.py:27
  142.0 14.5 %fusion.1 = f32[1024,128]{1,0:T(8,128)S(1)} fusion(bf16[1024,128]{1,0:T(8,128)(2,1)S(1)} %copy-done.4, bf16[1024,4096]{1,0:T(8,128)(2,1)} %multiply_convert_fusion, bf16[4096,1024]{1,0:T(8,128)(2,1)} %param.14), kind=kOutput, calls=%fused_computation.10 | convolution fusion | flops 8863612928 | bytes 17563648 | tf_op jit(solution)/shard_map/dot_general | solution.py:34
  156.6 0.8 copy.19
  157.4 4.2 %all-to-all-start.1 = ((f32[32,4,8,128]{3,2,1,0:T(8,128)}), f32[32,4,8,128]{3,2,1,0:T(8,128)S(1)}, u32[]{:S(2)}, u32[]{:S(2)}) async-start(f32[32,4,8,128]{3,2,1,0:T(8,128)} %bitcast.47), calls=%async_computation.1 | async-start | bytes 1048576 | tf_op jit(solution)/shard_map/all_to_all | solution.py:99
  161.7 16.2 %all-to-all-done.1 = f32[32,4,8,128]{3,2,1,0:T(8,128)S(1)} async-done(((f32[32,4,8,128]{3,2,1,0:T(8,128)}), f32[32,4,8,128]{3,2,1,0:T(8,128)S(1)}, u32[]{:S(2)}, u32[]{:S(2)}) %all-to-all-start.1) | async-done | bytes 524320 | tf_op jit(solution)/shard_map/all_to_all | solution.py:99
  178.0 0.7 gather_fusion.2
  178.7 0.7 select_convert_fusion
  (26 shorter events, 1.9 us)
Async XLA Ops:
  6.5 3.0 %copy-start = (bf16[2048,128]{1,0:T(8,128)(2,1)S(1)}, bf16[2048,128]{1,0:T(8,128)(2,1)}, u32[]{:S(2)}) copy-start(bf16[2048,128]{1,0:T(8,128)(2,1)} %param.9) | copy-start | bytes 1572868
  6.5 63.6 %all-gather.2.cloned.1.call-start = ((), (), s32[]{:S(2)}) async-start(), calls=%async_computation.2 | async-start | bytes 5242880 | tf_op jit(solution)/shard_map/all_gather | solution.py:56
  14.8 23.7 %all-to-all-start = ((bf16[32,32,129]{2,1,0:T(8,128)(2,1)}), bf16[32,32,129]{2,1,0:T(8,128)(2,1)S(1)}, u32[]{:S(2)}, u32[]{:S(2)}) async-start(bf16[32,32,129]{2,1,0:T(8,128)(2,1)} %bitcast.5), calls=%async_computation | async-start | bytes 1048576 | tf_op jit(solution)/shard_map/all_to_all | solution.py:79
  74.6 10.1 %copy-start.4 = (bf16[1024,128]{1,0:T(8,128)(2,1)S(1)}, bf16[1024,128]{1,0:T(8,128)(2,1)}, u32[]{:S(2)}) copy-start(bf16[1024,128]{1,0:T(8,128)(2,1)} %param.15) | copy-start | bytes 786436
  84.8 41.6 %copy-start.2 = (bf16[128,128]{1,0:T(8,128)(2,1)S(1)}, bf16[128,128]{1,0:T(8,128)(2,1)}, u32[]{:S(2)}) copy-start(bf16[128,128]{1,0:T(8,128)(2,1)} %param.17) | copy-start | bytes 98308
  142.0 19.7 %copy-start.3 = (s32[128,1]{0,1:T(1,128)S(1)}, s32[128,1]{0,1:T(1,128)}, u32[]{:S(2)}) copy-start(s32[128,1]{0,1:T(1,128)} %param.12) | copy-start | bytes 1540
  142.0 37.3 %copy-start.1 = (bf16[2048,128]{1,0:T(8,128)(2,1)S(1)}, bf16[2048,128]{1,0:T(8,128)(2,1)}, u32[]{:S(2)}) copy-start(bf16[2048,128]{1,0:T(8,128)(2,1)} %param.9) | copy-start | bytes 1572868
  157.4 20.5 %all-to-all-start.1 = ((f32[32,4,8,128]{3,2,1,0:T(8,128)}), f32[32,4,8,128]{3,2,1,0:T(8,128)S(1)}, u32[]{:S(2)}, u32[]{:S(2)}) async-start(f32[32,4,8,128]{3,2,1,0:T(8,128)} %bitcast.47), calls=%async_computation.1 | async-start | bytes 1048576 | tf_op jit(solution)/shard_map/all_to_all | solution.py:99
Sparse Core Ops, SparseCore 0:
  9.2 60.9 all-gather.1
where the time goes:
time: 187 us; the launch traced here: 186 us
  waiting for transfers between devices  63.6 us (34%)
  matrix products  48.6 us (26%)
  blocking collectives  27.1 us (14%)
  other arithmetic  16.8 us (9%)
  between operations  13.5 us (7%)
  starting transfers between devices  11.6 us (6%)
  local copies, waits for them, and re-layouts  5.03 us (3%)
    all_gather x1, waiting for transfers between devices, per_device(): lax.all_gather(first_layers, 'sec', axis=0, tiled=True)  31.4 us
    dot_general x2, matrix products, surrogate_tail(): return jnp.dot(middle, out_weight, preferred_element_type=jnp.float32)  29.1 us
    psum x1, blocking collectives, per_device(): values = lax.psum(partial, 'sec').astype(jnp.bfloat16)  27.1 us
    all_to_all x1, waiting for transfers between devices, per_device(): lax.all_to_all(back, ('sec', 'dev'), split_axis=0, concat_axis=0, tiled=T...  16.2 us
    all_to_all x1, waiting for transfers between devices, per_device(): lax.all_to_all(send, ('sec', 'dev'), split_axis=0, concat_axis=0, tiled=T...  15.2 us
    convert_element_type x1, other arithmetic, first_hidden(): return jax.nn.silu(mixed).astype(jnp.bfloat16)  10.9 us
    dot_general x1, matrix products, band_rows(): return jnp.dot(picks, parts, preferred_element_type=jnp.float32)  10.1 us
    dot_general x2, matrix products, first_hidden(): jnp.einsum('srf,sfh->srh', rows, weights, preferred_element_type=jnp.floa...  9.05 us
  transfers between devices with their start and end apart: 3, of which 3 were waited for; matrix products, arithmetic and copies ran while one was open for 5% of the time, Pallas kernels for 0%

commit v1 on v0

--- a/solution.py
+++ b/solution.py
@@ -86,7 +86,8 @@
         hidden = first_hidden(rows, every_first, got_band, parts)
         partial = surrogate_tail(hidden, middle_weight, out_weight)
         if segment_index + 1 < PASSES:
-            values = lax.psum(partial, "sec").astype(jnp.bfloat16)
+            find_stocks = lambda xs: jax.lax.all_gather(xs, axis_name="sec").sum(axis=0)
+            values = find_stocks(partial).astype(jnp.bfloat16)
             rows = (
                 rows.astype(jnp.float32)
                 + jnp.dot(values, back_weight, preferred_element_type=jnp.float32).reshape(

time: 187 us -> 199 us (1.064)
  waiting for transfers between devices: 63.6 us -> 98.9 us
  blocking collectives: 27.1 us -> 0 us
    all_gather x0 -> x1, waiting for transfers between devices: none -> 35.3 us  [per_device(): find_stocks = lambda xs: jax.lax.all_gather(xs, axis_name='sec').sum(axis=0)]
    psum x1 -> x0, blocking collectives: 27.1 us -> none  [per_device(): values = lax.psum(partial, 'sec').astype(jnp.bfloat16)]
  transfers between devices with their start and end apart: 3 -> 4, of which waited for: 3 -> 4; matrix products, arithmetic and copies ran while one was open for 5% -> 4% of each run, Pallas kernels for 0% -> 0%
where the time goes in v1:
time: 199 us
  waiting for transfers between devices  98.9 us (50%)
  matrix products  50.4 us (25%)
  other arithmetic  18.7 us (9%)
  between operations  13.5 us (7%)
  starting transfers between devices  12 us (6%)
  local copies, waits for them, and re-layouts  5.07 us (3%)
    all_gather x1, waiting for transfers between devices, per_device(): find_stocks = lambda xs: jax.lax.all_gather(xs, axis_name='sec').sum(axis=0)  35.3 us
    all_gather x1, waiting for transfers between devices, per_device(): lax.all_gather(first_layers, 'sec', axis=0, tiled=True)  31.4 us
    dot_general x2, matrix products, surrogate_tail(): return jnp.dot(middle, out_weight, preferred_element_type=jnp.float32)  30.6 us
    all_to_all x1, waiting for transfers between devices, per_device(): lax.all_to_all(back, ('sec', 'dev'), split_axis=0, concat_axis=0, tiled=T...  16.2 us
    all_to_all x1, waiting for transfers between devices, per_device(): lax.all_to_all(send, ('sec', 'dev'), split_axis=0, concat_axis=0, tiled=T...  15.2 us
    convert_element_type x1, other arithmetic, first_hidden(): return jax.nn.silu(mixed).astype(jnp.bfloat16)  11.1 us
    dot_general x1, matrix products, band_rows(): return jnp.dot(picks, parts, preferred_element_type=jnp.float32)  10.3 us
    dot_general x2, matrix products, first_hidden(): jnp.einsum('srf,sfh->srh', rows, weights, preferred_element_type=jnp.floa...  9.05 us
  transfers between devices with their start and end apart: 4, of which 4 were waited for; matrix products, arithmetic and copies ran while one was open for 4% of the time, Pallas kernels for 0%

profile of v1, /device:TPU:0, one launch (start us, length us, event | category | flops | bytes accessed | tf_op | source)
XLA Modules:
  0.0 198.5 jit_solution(3957255384183786157)
XLA Ops:
  6.5 0.7 all-gather.4.cloned.1.call-update
  7.9 1.6 gather_fusion.1
  9.6 0.7 gather_fusion
  11.1 0.7 fusion.22
  12.0 0.8 select_reduce_fusion
  12.8 0.7 fusion.28
  13.9 0.9 broadcast_in_dim.47
  14.8 7.3 %all-to-all-start = ((bf16[32,32,129]{2,1,0:T(8,128)(2,1)}), bf16[32,32,129]{2,1,0:T(8,128)(2,1)S(1)}, u32[]{:S(2)}, u32[]{:S(2)}) async-start(bf16[32,32,129]{2,1,0:T(8,128)(2,1)} %bitcast.5), calls=%async_computation | async-start | bytes 1048576 | tf_op jit(solution)/shard_map/all_to_all | solution.py:79
  22.2 1.1 fusion.33
  23.2 15.2 %all-to-all-done = bf16[32,32,129]{2,1,0:T(8,128)(2,1)S(1)} async-done(((bf16[32,32,129]{2,1,0:T(8,128)(2,1)}), bf16[32,32,129]{2,1,0:T(8,128)(2,1)S(1)}, u32[]{:S(2)}, u32[]{:S(2)}) %all-to-all-start) | async-done | bytes 264224 | tf_op jit(solution)/shard_map/all_to_all | solution.py:79
  38.7 31.4 %all-gather.4.cloned.1.call-done = bf16[512,4096]{1,0:T(8,128)(2,1)} async-done(((bf16[128,4096]{1,0:T(8,128)(2,1)}), bf16[512,4096]{1,0:T(8,128)(2,1)}) %all-gather.4.cloned.1.call-update) | async-done | bytes 4194320 | tf_op jit(solution)/shard_map/all_gather | solution.py:56
  70.1 4.5 %fusion.14 = f32[4,256,4096]{2,1,0:T(8,128)S(1)} fusion(bf16[4,128,4096]{2,1,0:T(8,128)(2,1)} %bitcast.49, bf16[4,256,129]{2,1,0:T(8,128)(2,1)S(1)} %copy_bitcast_fusion.1), kind=kOutput, calls=%fused_computation.30 | convolution fusion | flops 1073741824 | bytes 21233664 | tf_op jit(solution)/shard_map/srf,sfh->srh/dot_general | solution.py:25
  74.7 10.3 %multiply_convert_fusion.1 = (bf16[1024,4096]{1,0:T(8,128)(2,1)}, f32[1024,4096]{1,0:T(8,128)}) fusion(f32[4,256,4096]{2,1,0:T(8,128)S(1)} %fusion.14, bf16[16,4096]{1,0:T(8,128)(2,1)S(1)} %get-tuple-element.10, bf16[16,4096]{1,0:T(8,128)(2,1)S(1)} %get-tuple-element.11, bf16[16,4096]{1,0:T(8,128)(2,1)S(1)} %get-tuple-element.9, s32[48]{0:T(128)S(1)} %and_select_fusion, ...), kind=kOutput, calls=%fused_computation.6 | convolution fusion | flops 429047808 | bytes 42340544 | tf_op jit(solution)/shard_map/dot_general | solution.py:21
  84.9 16.1 %fusion = f32[1024,128]{1,0:T(8,128)} fusion(bf16[1024,128]{1,0:T(8,128)(2,1)S(1)} %copy-done.4, bf16[1024,4096]{1,0:T(8,128)(2,1)} %get-tuple-element.12, bf16[4096,1024]{1,0:T(8,128)(2,1)} %param.14), kind=kOutput, calls=%fused_computation.9 | convolution fusion | flops 8863612928 | bytes 17563648 | tf_op jit(solution)/shard_map/dot_general | solution.py:34
  101.0 35.3 %all-gather.6.cloned.1.call-done = f32[4096,128]{1,0:T(8,128)} async-done(((f32[1024,128]{1,0:T(8,128)}), f32[4096,128]{1,0:T(8,128)}) %all-gather.6.cloned.1.call-update) | async-done | bytes 2097168 | tf_op jit(solution)/shard_map/all_gather | solution.py:89
  136.4 1.7 reduce_sum.31
  138.3 4.5 %fusion.9 = f32[4,256,4096]{2,1,0:T(8,128)S(1)} fusion(bf16[4,128,4096]{2,1,0:T(8,128)(2,1)} %bitcast.50, f32[4,256,128]{2,1,0:T(8,128)S(1)} %bitcast.52, bf16[4,256,129]{2,1,0:T(8,128)(2,1)S(1)} %copy_bitcast_fusion.1), kind=kOutput, calls=%fused_computation.23 | convolution fusion | flops 1074135040 | bytes 21757952 | tf_op jit(solution)/shard_map/srf,sfh->srh/dot_general | solution.py:25
  142.9 11.1 %multiply_convert_fusion = bf16[1024,4096]{1,0:T(8,128)(2,1)} fusion(f32[1024,4096]{1,0:T(8,128)} %get-tuple-element.13, f32[4,256,4096]{2,1,0:T(8,128)S(1)} %fusion.9), kind=kLoop, calls=%fused_computation.5 | loop fusion | flops 25165824 | bytes 41943040 | tf_op jit(solution)/shard_map/convert_element_type | solution.py:27
  154.0 14.5 %fusion.1 = f32[1024,128]{1,0:T(8,128)S(1)} fusion(bf16[1024,128]{1,0:T(8,128)(2,1)S(1)} %copy-done.4, bf16[1024,4096]{1,0:T(8,128)(2,1)} %multiply_convert_fusion, bf16[4096,1024]{1,0:T(8,128)(2,1)} %param.14), kind=kOutput, calls=%fused_computation.10 | convolution fusion | flops 8863612928 | bytes 17563648 | tf_op jit(solution)/shard_map/dot_general | solution.py:34
  168.5 0.9 copy.19
  169.4 4.6 %all-to-all-start.1 = ((f32[32,4,8,128]{3,2,1,0:T(8,128)}), f32[32,4,8,128]{3,2,1,0:T(8,128)S(1)}, u32[]{:S(2)}, u32[]{:S(2)}) async-start(f32[32,4,8,128]{3,2,1,0:T(8,128)} %bitcast.48), calls=%async_computation.1 | async-start | bytes 1048576 | tf_op jit(solution)/shard_map/all_to_all | solution.py:100
  174.1 16.2 %all-to-all-done.1 = f32[32,4,8,128]{3,2,1,0:T(8,128)S(1)} async-done(((f32[32,4,8,128]{3,2,1,0:T(8,128)}), f32[32,4,8,128]{3,2,1,0:T(8,128)S(1)}, u32[]{:S(2)}, u32[]{:S(2)}) %all-to-all-start.1) | async-done | bytes 524320 | tf_op jit(solution)/shard_map/all_to_all | solution.py:100
  190.3 0.7 gather_fusion.2
  191.0 0.7 select_convert_fusion
  (29 shorter events, 2.6 us)
Async XLA Ops:
  6.5 3.0 %copy-start = (bf16[2048,128]{1,0:T(8,128)(2,1)S(1)}, bf16[2048,128]{1,0:T(8,128)(2,1)}, u32[]{:S(2)}) copy-start(bf16[2048,128]{1,0:T(8,128)(2,1)} %param.9) | copy-start | bytes 1572868
  6.5 63.6 %all-gather.4.cloned.1.call-start = ((), (), s32[]{:S(2)}) async-start(), calls=%async_computation.2 | async-start | bytes 5242880 | tf_op jit(solution)/shard_map/all_gather | solution.py:56
  14.8 23.7 %all-to-all-start = ((bf16[32,32,129]{2,1,0:T(8,128)(2,1)}), bf16[32,32,129]{2,1,0:T(8,128)(2,1)S(1)}, u32[]{:S(2)}, u32[]{:S(2)}) async-start(bf16[32,32,129]{2,1,0:T(8,128)(2,1)} %bitcast.5), calls=%async_computation | async-start | bytes 1048576 | tf_op jit(solution)/shard_map/all_to_all | solution.py:79
  22.1 114.3 %all-gather.6.cloned.1.call-start = ((), (), s32[]{:S(2)}) async-start(), calls=%async_computation.3 | async-start | bytes 2621440 | tf_op jit(solution)/shard_map/all_gather | solution.py:89
  74.6 10.3 %copy-start.4 = (bf16[1024,128]{1,0:T(8,128)(2,1)S(1)}, bf16[1024,128]{1,0:T(8,128)(2,1)}, u32[]{:S(2)}) copy-start(bf16[1024,128]{1,0:T(8,128)(2,1)} %param.15) | copy-start | bytes 786436
  84.9 53.2 %copy-start.2 = (bf16[128,128]{1,0:T(8,128)(2,1)S(1)}, bf16[128,128]{1,0:T(8,128)(2,1)}, u32[]{:S(2)}) copy-start(bf16[128,128]{1,0:T(8,128)(2,1)} %param.17) | copy-start | bytes 98308
  154.0 20.0 %copy-start.3 = (s32[128,1]{0,1:T(1,128)S(1)}, s32[128,1]{0,1:T(1,128)}, u32[]{:S(2)}) copy-start(s32[128,1]{0,1:T(1,128)} %param.12) | copy-start | bytes 1540
  154.0 37.7 %copy-start.1 = (bf16[2048,128]{1,0:T(8,128)(2,1)S(1)}, bf16[2048,128]{1,0:T(8,128)(2,1)}, u32[]{:S(2)}) copy-start(bf16[2048,128]{1,0:T(8,128)(2,1)} %param.9) | copy-start | bytes 1572868
  169.4 20.8 %all-to-all-start.1 = ((f32[32,4,8,128]{3,2,1,0:T(8,128)}), f32[32,4,8,128]{3,2,1,0:T(8,128)S(1)}, u32[]{:S(2)}, u32[]{:S(2)}) async-start(f32[32,4,8,128]{3,2,1,0:T(8,128)} %bitcast.48), calls=%async_computation.1 | async-start | bytes 1048576 | tf_op jit(solution)/shard_map/all_to_all | solution.py:100
Sparse Core Ops, SparseCore 0:
  9.2 60.9 all-gather.3
  101.2 35.1 all-gather.5
